TPU v7x, 128 devices: a whole 4x4x4 slice. The times are simulated.
128 devices in a mesh: expert: 4 (over z_lo, core), fsdp: 32 (over y, z_hi, x).
Axes of the slice: x: 4, y: 4, z: 4 (z_hi: 2, z_lo: 2; z = z_hi * 2 + z_lo), core: 2. Of those that a mesh axis runs over, the one named last changes fastest.
Arguments:
- tokens: bfloat16 [16384, 2048], P(('expert', 'fsdp')), may hold values from -6 to 6
- expert_ids: int32 [16384, 1], P(('expert', 'fsdp')), may hold values from 0 to 7; in each aligned block of 128 rows (0 to 127, 128 to 255, ...) at most 24 rows name the same one
- gate_weight: bfloat16 [8, 2048, 8192], P('expert', None, 'fsdp'), may hold values from -0.125 to 0.125
- up_weight: bfloat16 [8, 2048, 8192], P('expert', None, 'fsdp'), may hold values from -0.125 to 0.125
- hidden_grad: bfloat16 [8, 3072, 8192], P('expert', None, 'fsdp'), may hold values from -0.1796875 to 0.1796875
Outputs:
- hidden: bfloat16 [8, 3072, 8192], P('expert', None, 'fsdp')
- gate_grad: float32 [8, 2048, 8192], P('expert', None, 'fsdp')
- up_grad: float32 [8, 2048, 8192], P('expert', None, 'fsdp')
Inputs may be any that keep to these rules, and one draw needn't show every extreme that they name: `expert_ids`: within the tokens of one device (aligned blocks of 128 rows) no expert is named more than 24 times, a bound that some block reaches.
All inputs are finite; a program needn't handle non-finite values.
Results may differ from a plain program's by a relative error of at most 0.003.
Values may be sent and summed in bfloat16 or wider, within the bound.
No kernel may reach another device: no remote copies, remote signals or barrier semaphores. Data moves between devices by JAX's collectives and lax.ppermute only.
A program may use at most 192 MiB of HBM per device.

v0:
```python
import jax
import jax.numpy as jnp
from jax import lax
from jax.sharding import PartitionSpec as P

CAP = 24


def chunk_pass(rows, gate_w, up_w, cotan):
    gate = jnp.einsum("grd,gdf->grf", rows, gate_w, preferred_element_type=jnp.float32)
    upval = jnp.einsum("grd,gdf->grf", rows, up_w, preferred_element_type=jnp.float32)
    cotan = cotan.astype(jnp.float32)
    sigma = 1.0 / (1.0 + jnp.exp(-gate))
    active = gate * sigma
    hidden = (active * upval).astype(jnp.bfloat16)
    gate_delta = (cotan * upval * sigma * (1.0 + gate * (1.0 - sigma))).astype(jnp.bfloat16)
    up_delta = (cotan * active).astype(jnp.bfloat16)
    gate_sum = jnp.einsum("grd,grf->gdf", rows, gate_delta, preferred_element_type=jnp.float32)
    up_sum = jnp.einsum("grd,grf->gdf", rows, up_delta, preferred_element_type=jnp.float32)
    return (hidden, gate_sum, up_sum)


def on_device(tokens, expert_ids, gate_weight, up_weight, hidden_grad):
    owners = lax.axis_size("expert")
    members = lax.axis_size("fsdp")
    per_owner = gate_weight.shape[0]
    model = gate_weight.shape[1]
    route = expert_ids[:, 0]
    total_experts = per_owner * owners
    onehot = (route[:, None] == jnp.arange(total_experts, dtype=jnp.int32)[None, :]).astype(
        jnp.int32
    )
    rank = jnp.sum((jnp.cumsum(onehot, axis=0) - onehot) * onehot, axis=1)
    owner_of = route // per_owner
    within = route % per_owner
    target = owner_of * (per_owner * CAP) + within * CAP + rank
    send_rows = per_owner * owners * CAP
    placing = (jnp.arange(send_rows, dtype=jnp.int32)[:, None] == target[None, :]).astype(
        jnp.bfloat16
    )
    outgoing = jnp.dot(placing, tokens, preferred_element_type=jnp.float32).astype(jnp.bfloat16)
    outgoing = outgoing.reshape(owners, per_owner, CAP, model)
    arrived = lax.all_to_all(outgoing, "expert", split_axis=0, concat_axis=0, tiled=True)
    slot_count = members * CAP

    def gather(source):
        piece = lax.dynamic_index_in_dim(arrived, source, axis=0, keepdims=False)
        return lax.all_gather(piece, "fsdp", axis=1, tiled=True)

    def step(source, rows, hidden_buf, gate_acc, up_acc):
        start = source * slot_count
        cotan = lax.dynamic_slice_in_dim(hidden_grad, start, slot_count, axis=1)
        hidden, gate_sum, up_sum = chunk_pass(rows, gate_weight, up_weight, cotan)
        hidden_buf = lax.dynamic_update_slice_in_dim(hidden_buf, hidden, start, axis=1)
        return (hidden_buf, gate_acc + gate_sum, up_acc + up_sum)

    def body(source, carry):
        rows, hidden_buf, gate_acc, up_acc = carry
        next_rows = gather(source + 1)
        hidden_buf, gate_acc, up_acc = step(source, rows, hidden_buf, gate_acc, up_acc)
        return (next_rows, hidden_buf, gate_acc, up_acc)

    hidden_buf = jnp.zeros(hidden_grad.shape, jnp.bfloat16)
    gate_acc = jnp.zeros(gate_weight.shape, jnp.float32)
    up_acc = jnp.zeros(up_weight.shape, jnp.float32)
    rows = gather(0)
    rows, hidden_buf, gate_acc, up_acc = lax.fori_loop(
        0, owners - 1, body, (rows, hidden_buf, gate_acc, up_acc)
    )
    hidden_buf, gate_acc, up_acc = step(owners - 1, rows, hidden_buf, gate_acc, up_acc)
    return (hidden_buf, gate_acc, up_acc)


def solution(mesh):
    in_specs = (
        P(("expert", "fsdp"), None),
        P(("expert", "fsdp"), None),
        P("expert", None, "fsdp"),
        P("expert", None, "fsdp"),
        P("expert", None, "fsdp"),
    )
    out_specs = (P("expert", None, "fsdp"), P("expert", None, "fsdp"), P("expert", None, "fsdp"))
    return jax.shard_map(
        on_device, mesh=mesh, in_specs=in_specs, out_specs=out_specs, check_vma=False
    )
```

profile of v0, /device:TPU:1, one launch (start us, length us, event | category | flops | bytes accessed | tf_op | source)
XLA Modules:
  0.0 467.2 jit_solution(2851810721346810936)
XLA Ops:
  7.2 0.8 fusion.28
  8.2 0.8 select_reduce_fusion
  10.1 15.1 %all_to_all.5 = bf16[4,2,24,2048]{3,2,1,0:T(8,128)(2,1)S(1)} all-to-all(bf16[4,2,24,2048]{3,2,1,0:T(8,128)(2,1)S(1)} %bitcast.46), channel_id=1, replica_groups=mesh['expert'=4,'fsdp'=32] {'expert'}, dimensions={0} | all-to-all | bytes 1572864 | tf_op jit(solution)/shard_map/all_to_all | solution.py:43
  25.9 94.5 %all-gather.8.cloned.1.call-done = bf16[1,2,768,2048]{3,2,1,0:T(8,128)(2,1)} async-done(((bf16[1,2,24,2048]{3,2,1,0:T(8,128)(2,1)}), bf16[1,2,768,2048]{3,2,1,0:T(8,128)(2,1)}) %all-gather.8.cloned.1.call-update) | async-done | bytes 6291472 | tf_op jit(solution)/shard_map/all_gather | solution.py:48
  120.4 1.9 broadcast_in_dim.2
  122.3 301.8 %while.22 = (s32[]{:T(128)}, bf16[2,768,2048]{2,1,0:T(8,128)(2,1)}, bf16[2,3072,256]{2,1,0:T(8,128)(2,1)}, f32[2,2048,256]{1,2,0:T(8,128)}, f32[2,2048,256]{1,2,...) while((s32[]{:T(128)}, bf16[2,768,2048]{2,1,0:T(8,128)(2,1)}, ...), condition=%wide.region_3.4_spmd.clone, body=%wide.region_2.3_spmd.clone.sunk | while | flops 6456082432 | bytes 130220424 | solution.py:67
  123.0 5.3 %fusion.68 = f32[2,768,256]{2,1,0:T(8,128)S(1)} fusion(bf16[2,768,2048]{2,1,0:T(8,128)(2,1)} %get-tuple-element.356, bf16[2,2048,256]{2,1,0:T(8,128)(2,1)} %get-tuple-element.375), kind=kOutput, calls=%fused_computation.51.clone.1 | convolution fusion | flops 1610612736 | bytes 9961472 | tf_op jit(solution)/shard_map/while/body/eval_jaxpr/grd,gdf->grf/dot_general | solution.py:10
  128.8 2.9 fusion.69
  131.8 4.1 bitcast_add_fusion.5
  135.9 4.4 bitcast_add_fusion.4
  140.3 76.2 %all-gather.10.cloned.1.call-done = bf16[1,2,768,2048]{3,2,1,0:T(8,128)(2,1)} async-done(((bf16[1,2,24,2048]{3,2,1,0:T(8,128)(2,1)}), bf16[1,2,768,2048]{3,2,1,0:T(8,128)(2,1)}) %all-gather.10.cloned.1.call-update) | async-done | bytes 6291472 | tf_op jit(solution)/shard_map/while/body/eval_jaxpr/all_gather | solution.py:48
  216.4 6.6 %copy.30 = bf16[2,768,2048]{2,1,0:T(8,128)(2,1)} copy(bf16[2,768,2048]{2,1,0:T(8,128)(2,1)} %bitcast.40) | data formatting | bytes 12582912 | tf_op jit(solution)/shard_map/while
  223.0 0.7 constant_dynamic-slice_fusion.2
  223.7 5.3 %fusion.68 = f32[2,768,256]{2,1,0:T(8,128)S(1)} fusion(bf16[2,768,2048]{2,1,0:T(8,128)(2,1)} %get-tuple-element.356, bf16[2,2048,256]{2,1,0:T(8,128)(2,1)} %get-tuple-element.375), kind=kOutput, calls=%fused_computation.51.clone.1 | convolution fusion | flops 1610612736 | bytes 9961472 | tf_op jit(solution)/shard_map/while/body/eval_jaxpr/grd,gdf->grf/dot_general | solution.py:10
  229.5 2.9 fusion.69
  232.5 6.3 %bitcast_add_fusion.5 = f32[2,2048,256]{1,2,0:T(8,128)} fusion(f32[2,2048,256]{1,2,0:T(8,128)} %get-tuple-element.359, bf16[2,768,2048]{2,1,0:T(8,128)(2,1)S(1)} %bitcast.43, pred[]{:T(512)S(6)} %compare.14, bf16[2,3072,256]{2,1,0:T(8,128)(2,1)S(1)} %copy-done.4, s32[]{:T(128)S(6)} %select_n.61, f32[2,768,256]{2,1,0:T(8,128)S(1)} %fusion.68), kind=kOutput, calls=%fused_computation.clone.1 | convolution fusion | flops 1615462400 | bytes 17039364 | tf_op jit(solution)/shard_map/while/body/eval_jaxpr/grd,grf->gdf/dot_general | solution.py:19
  238.8 6.6 %bitcast_add_fusion.4 = f32[2,2048,256]{1,2,0:T(8,128)} fusion(f32[2,2048,256]{1,2,0:T(8,128)} %get-tuple-element.358, bf16[2,768,2048]{2,1,0:T(8,128)(2,1)S(1)} %bitcast.43, pred[]{:T(512)S(6)} %compare.14, f32[2,768,256]{2,1,0:T(8,128)S(1)} %get-tuple-element.340, f32[2,768,256]{2,1,0:T(8,128)S(1)} %fusion.68, ...), kind=kOutput, calls=%fused_computation.1.clone.1 | convolution fusion | flops 1617035264 | bytes 18612228 | tf_op jit(solution)/shard_map/while/body/eval_jaxpr/grd,grf->gdf/dot_general | solution.py:18
  245.3 71.8 %all-gather.10.cloned.1.call-done = bf16[1,2,768,2048]{3,2,1,0:T(8,128)(2,1)} async-done(((bf16[1,2,24,2048]{3,2,1,0:T(8,128)(2,1)}), bf16[1,2,768,2048]{3,2,1,0:T(8,128)(2,1)}) %all-gather.10.cloned.1.call-update) | async-done | bytes 6291472 | tf_op jit(solution)/shard_map/while/body/eval_jaxpr/all_gather | solution.py:48
  317.1 6.6 %copy.30 = bf16[2,768,2048]{2,1,0:T(8,128)(2,1)} copy(bf16[2,768,2048]{2,1,0:T(8,128)(2,1)} %bitcast.40) | data formatting | bytes 12582912 | tf_op jit(solution)/shard_map/while
  323.7 0.7 constant_dynamic-slice_fusion.2
  324.4 5.3 %fusion.68 = f32[2,768,256]{2,1,0:T(8,128)S(1)} fusion(bf16[2,768,2048]{2,1,0:T(8,128)(2,1)} %get-tuple-element.356, bf16[2,2048,256]{2,1,0:T(8,128)(2,1)} %get-tuple-element.375), kind=kOutput, calls=%fused_computation.51.clone.1 | convolution fusion | flops 1610612736 | bytes 9961472 | tf_op jit(solution)/shard_map/while/body/eval_jaxpr/grd,gdf->grf/dot_general | solution.py:10
  330.2 2.9 fusion.69
  333.2 6.3 %bitcast_add_fusion.5 = f32[2,2048,256]{1,2,0:T(8,128)} fusion(f32[2,2048,256]{1,2,0:T(8,128)} %get-tuple-element.359, bf16[2,768,2048]{2,1,0:T(8,128)(2,1)S(1)} %bitcast.43, pred[]{:T(512)S(6)} %compare.14, bf16[2,3072,256]{2,1,0:T(8,128)(2,1)S(1)} %copy-done.4, s32[]{:T(128)S(6)} %select_n.61, f32[2,768,256]{2,1,0:T(8,128)S(1)} %fusion.68), kind=kOutput, calls=%fused_computation.clone.1 | convolution fusion | flops 1615462400 | bytes 17039364 | tf_op jit(solution)/shard_map/while/body/eval_jaxpr/grd,grf->gdf/dot_general | solution.py:19
  339.4 6.6 %bitcast_add_fusion.4 = f32[2,2048,256]{1,2,0:T(8,128)} fusion(f32[2,2048,256]{1,2,0:T(8,128)} %get-tuple-element.358, bf16[2,768,2048]{2,1,0:T(8,128)(2,1)S(1)} %bitcast.43, pred[]{:T(512)S(6)} %compare.14, f32[2,768,256]{2,1,0:T(8,128)S(1)} %get-tuple-element.340, f32[2,768,256]{2,1,0:T(8,128)S(1)} %fusion.68, ...), kind=kOutput, calls=%fused_computation.1.clone.1 | convolution fusion | flops 1617035264 | bytes 18612228 | tf_op jit(solution)/shard_map/while/body/eval_jaxpr/grd,grf->gdf/dot_general | solution.py:18
  346.0 71.5 %all-gather.10.cloned.1.call-done = bf16[1,2,768,2048]{3,2,1,0:T(8,128)(2,1)} async-done(((bf16[1,2,24,2048]{3,2,1,0:T(8,128)(2,1)}), bf16[1,2,768,2048]{3,2,1,0:T(8,128)(2,1)}) %all-gather.10.cloned.1.call-update) | async-done | bytes 6291472 | tf_op jit(solution)/shard_map/while/body/eval_jaxpr/all_gather | solution.py:48
  417.5 6.6 %copy.30 = bf16[2,768,2048]{2,1,0:T(8,128)(2,1)} copy(bf16[2,768,2048]{2,1,0:T(8,128)(2,1)} %bitcast.40) | data formatting | bytes 12582912 | tf_op jit(solution)/shard_map/while
  424.1 5.5 %copy.13 = f32[2,2048,256]{2,1,0:T(8,128)} copy(f32[2,2048,256]{1,2,0:T(8,128)} %get-tuple-element.229) | data formatting | bytes 8388608 | tf_op jit(solution)/shard_map/while | solution.py:67
  429.6 5.3 %fusion.36 = f32[2,768,256]{2,1,0:T(8,128)S(1)} fusion(bf16[2,768,2048]{2,1,0:T(8,128)(2,1)} %get-tuple-element.227, bf16[2,2048,256]{2,1,0:T(8,128)(2,1)} %get-tuple-element.392), kind=kOutput, calls=%fused_computation.52 | convolution fusion | flops 1610612736 | bytes 9961472 | tf_op jit(solution)/shard_map/grd,gdf->grf/dot_general | solution.py:10
  435.5 6.7 %convolution_add_fusion = f32[2,2048,256]{2,1,0:T(8,128)} fusion(f32[2,2048,256]{2,1,0:T(8,128)S(1)} %copy-done.1, bf16[2,768,2048]{2,1,0:T(8,128)(2,1)S(1)} %bitcast.45, bf16[2,3072,256]{2,1,0:T(8,128)(2,1)} %get-tuple-element.389, f32[2,768,256]{2,1,0:T(8,128)S(1)} %fusion.36), kind=kOutput, calls=%fused_computation.20 | convolution fusion | flops 1614413824 | bytes 17039360 | tf_op jit(solution)/shard_map/grd,grf->gdf/dot_general | solution.py:19
  442.2 3.4 fusion.21
  445.6 5.5 %copy.11 = f32[2,2048,256]{2,1,0:T(8,128)} copy(f32[2,2048,256]{1,2,0:T(8,128)} %get-tuple-element.228) | data formatting | bytes 8388608 | tf_op jit(solution)/shard_map/while | solution.py:67
  451.1 9.6 %convolution_add_fusion.1 = f32[2,2048,256]{2,1,0:T(8,128)} fusion(f32[2,2048,256]{2,1,0:T(8,128)} %copy.11, bf16[2,768,2048]{2,1,0:T(8,128)(2,1)} %get-tuple-element.227, f32[2,768,256]{2,1,0:T(8,128)} %get-tuple-element.281, f32[2,768,256]{2,1,0:T(8,128)S(1)} %copy-done.3, bf16[2,3072,256]{2,1,0:T(8,128)(2,1)} %get-tuple-element.389), kind=kOutput, calls=%fused_computation.21 | convolution fusion | flops 1615986688 | bytes 18612224 | tf_op jit(solution)/shard_map/grd,grf->gdf/dot_general | solution.py:18
  (57 shorter events, 4.6 us)
Async XLA Ops:
  7.2 2.5 copy-start
  7.2 113.2 %all-gather.8.cloned.1.call-start = ((), (), s32[]{:S(2)}) async-start(), calls=%async_computation.1 | async-start | bytes 6488064 | tf_op jit(solution)/shard_map/all_gather | solution.py:48
  122.3 94.1 %all-gather.10.cloned.1.call-start = ((), (), s32[]{:S(2)}) async-start(), calls=%async_computation.2 | async-start | bytes 6488064 | tf_op jit(solution)/shard_map/while/body/eval_jaxpr/all_gather | solution.py:48
  123.0 5.4 %slice-start = ((s8[6291456]{0:T(1024)(128)(4,1)}), s8[2097152]{0:T(1024)(128)(4,1)S(1)}, s32[]{:S(2)}) async-start(s8[6291456]{0:T(1024)(128)(4,1)} %bitcast.42), calls=%async_computation.3 | async-start | bytes 4194304 | tf_op jit(solution)/shard_map/while
  123.0 5.4 %slice-start.1 = ((s8[6291456]{0:T(1024)(128)(4,1)}), s8[4194304]{0:T(1024)(128)(4,1)S(1)}, s32[]{:S(2)}) async-start(s8[6291456]{0:T(1024)(128)(4,1)} %bitcast.42), calls=%async_computation.4 | async-start | bytes 8388608 | tf_op jit(solution)/shard_map/while
  123.0 5.8 %copy-start.5 = (bf16[2,2048,256]{2,1,0:T(8,128)(2,1)S(1)}, bf16[2,2048,256]{2,1,0:T(8,128)(2,1)}, u32[]{:S(2)}) copy-start(bf16[2,2048,256]{2,1,0:T(8,128)(2,1)} %get-tuple-element.376) | copy-start | bytes 6291460 | tf_op jit(solution)/shard_map/while
  128.8 2.9 copy-start.4
  223.0 94.1 %all-gather.10.cloned.1.call-start = ((), (), s32[]{:S(2)}) async-start(), calls=%async_computation.2 | async-start | bytes 6488064 | tf_op jit(solution)/shard_map/while/body/eval_jaxpr/all_gather | solution.py:48
  223.7 5.4 %slice-start = ((s8[6291456]{0:T(1024)(128)(4,1)}), s8[2097152]{0:T(1024)(128)(4,1)S(1)}, s32[]{:S(2)}) async-start(s8[6291456]{0:T(1024)(128)(4,1)} %bitcast.42), calls=%async_computation.3 | async-start | bytes 4194304 | tf_op jit(solution)/shard_map/while
  223.7 5.4 %slice-start.1 = ((s8[6291456]{0:T(1024)(128)(4,1)}), s8[4194304]{0:T(1024)(128)(4,1)S(1)}, s32[]{:S(2)}) async-start(s8[6291456]{0:T(1024)(128)(4,1)} %bitcast.42), calls=%async_computation.4 | async-start | bytes 8388608 | tf_op jit(solution)/shard_map/while
  223.7 5.8 %copy-start.5 = (bf16[2,2048,256]{2,1,0:T(8,128)(2,1)S(1)}, bf16[2,2048,256]{2,1,0:T(8,128)(2,1)}, u32[]{:S(2)}) copy-start(bf16[2,2048,256]{2,1,0:T(8,128)(2,1)} %get-tuple-element.376) | copy-start | bytes 6291460 | tf_op jit(solution)/shard_map/while
  229.5 2.9 copy-start.4
  323.7 93.8 %all-gather.10.cloned.1.call-start = ((), (), s32[]{:S(2)}) async-start(), calls=%async_computation.2 | async-start | bytes 6488064 | tf_op jit(solution)/shard_map/while/body/eval_jaxpr/all_gather | solution.py:48
  324.4 5.4 %slice-start = ((s8[6291456]{0:T(1024)(128)(4,1)}), s8[2097152]{0:T(1024)(128)(4,1)S(1)}, s32[]{:S(2)}) async-start(s8[6291456]{0:T(1024)(128)(4,1)} %bitcast.42), calls=%async_computation.3 | async-start | bytes 4194304 | tf_op jit(solution)/shard_map/while
  324.4 5.4 %slice-start.1 = ((s8[6291456]{0:T(1024)(128)(4,1)}), s8[4194304]{0:T(1024)(128)(4,1)S(1)}, s32[]{:S(2)}) async-start(s8[6291456]{0:T(1024)(128)(4,1)} %bitcast.42), calls=%async_computation.4 | async-start | bytes 8388608 | tf_op jit(solution)/shard_map/while
  324.4 5.8 %copy-start.5 = (bf16[2,2048,256]{2,1,0:T(8,128)(2,1)S(1)}, bf16[2,2048,256]{2,1,0:T(8,128)(2,1)}, u32[]{:S(2)}) copy-start(bf16[2,2048,256]{2,1,0:T(8,128)(2,1)} %get-tuple-element.376) | copy-start | bytes 6291460 | tf_op jit(solution)/shard_map/while
  330.2 2.9 copy-start.4
  424.1 10.9 %slice-start.2 = ((s8[6291456]{0:T(1024)(128)(4,1)}), s8[2097152]{0:T(1024)(128)(4,1)S(1)}, s32[]{:S(2)}) async-start(s8[6291456]{0:T(1024)(128)(4,1)} %bitcast.44), calls=%async_computation.5 | async-start | bytes 4194304
  429.6 5.4 %slice-start.3 = ((s8[6291456]{0:T(1024)(128)(4,1)}), s8[4194304]{0:T(1024)(128)(4,1)S(1)}, s32[]{:S(2)}) async-start(s8[6291456]{0:T(1024)(128)(4,1)} %bitcast.44), calls=%async_computation.6 | async-start | bytes 8388608
  429.6 5.9 %copy-start.1 = (f32[2,2048,256]{2,1,0:T(8,128)S(1)}, f32[2,2048,256]{2,1,0:T(8,128)}, u32[]{:S(2)}) copy-start(f32[2,2048,256]{2,1,0:T(8,128)} %copy.13) | copy-start | bytes 12582916
  435.5 6.7 %copy-start.2 = (f32[2,768,256]{2,1,0:T(8,128)}, f32[2,768,256]{2,1,0:T(8,128)S(1)}, u32[]{:S(2)}) copy-start(f32[2,768,256]{2,1,0:T(8,128)S(1)} %fusion.36) | copy-start | bytes 4718596
  435.5 6.7 %copy-start.6 = (bf16[2,2048,256]{2,1,0:T(8,128)(2,1)S(1)}, bf16[2,2048,256]{2,1,0:T(8,128)(2,1)}, u32[]{:S(2)}) copy-start(bf16[2,2048,256]{2,1,0:T(8,128)(2,1)} %get-tuple-element.393) | copy-start | bytes 6291460
  445.6 5.5 %copy-start.3 = (f32[2,768,256]{2,1,0:T(8,128)S(1)}, f32[2,768,256]{2,1,0:T(8,128)}, u32[]{:S(2)}) copy-start(f32[2,768,256]{2,1,0:T(8,128)} %copy-done.2) | copy-start | bytes 4718596
Sparse Core Ops, SparseCore 0:
  26.0 94.3 all-gather.7
  126.2 90.1 all-gather.9
  226.9 90.1 all-gather.9
  327.3 90.1 all-gather.9
where the time goes:
time: 468 us; the launch traced here: 467 us
  waiting for transfers between devices  314 us (67%)
  matrix products  84.4 us (18%)
  local copies, waits for them, and re-layouts  37.3 us (8%)
  blocking collectives  15.1 us (3%)
  between operations  13.8 us (3%)
    all_gather x4, waiting for transfers between devices, gather(): return lax.all_gather(piece, 'fsdp', axis=1, tiled=True)  314 us
    dot_general x4, matrix products, chunk_pass(): jnp.einsum('grd,grf->gdf', rows, gate_delta, preferred_element_type=jnp.f...  27.2 us
    dot_general x4, matrix products, chunk_pass(): jnp.einsum('grd,grf->gdf', rows, up_delta, preferred_element_type=jnp.flo...  23.4 us
    dot_general x4, matrix products, chunk_pass(): jnp.einsum('grd,gdf->grf', rows, gate_w, preferred_element_type=jnp.float32)  21.4 us
    while x27, local copies, waits for them, and re-layouts  21 us
    all_to_all x1, blocking collectives, on_device(): lax.all_to_all(outgoing, 'expert', split_axis=0, concat_axis=0, tiled=True)  15.1 us
    dot_general x4, matrix products, chunk_pass(): jnp.einsum('grd,gdf->grf', rows, up_w, preferred_element_type=jnp.float32)  12.2 us
    while x2, local copies, waits for them, and re-layouts, on_device(): lax.fori_loop(0, owners - 1, body, (rows, hidden_buf, gate_acc, up_acc))  11 us
  transfers between devices with their start and end apart: 4, of which 4 were waited for; matrix products, arithmetic and copies ran while one was open for 13% of the time, Pallas kernels for 0%

commit v1 on v0

--- a/solution.py
+++ b/solution.py
@@ -45,7 +45,9 @@
 
     def gather(source):
         piece = lax.dynamic_index_in_dim(arrived, source, axis=0, keepdims=False)
-        return lax.all_gather(piece, "fsdp", axis=1, tiled=True)
+        return jnp.concatenate(
+            lax.all_to_all(jnp.stack([piece] * lax.axis_size("fsdp")), "fsdp", 0, 0), axis=1
+        )
 
     def step(source, rows, hidden_buf, gate_acc, up_acc):
         start = source * slot_count

time: 468 us -> 471 us (level)
  the two profiles are of different devices: /device:TPU:1 before, /device:TPU:4 now
where the time goes in v1:
time: 471 us; the launch traced here: 470 us
  waiting for transfers between devices  279 us (59%)
  matrix products  91.9 us (20%)
  local copies, waits for them, and re-layouts  54.2 us (12%)
  starting transfers between devices  27.5 us (6%)
  blocking collectives  14.6 us (3%)
    all_to_all x4, waiting for transfers between devices, gather(): lax.all_to_all(jnp.stack([piece] * lax.axis_size('fsdp')), 'fsdp', 0, 0)  279 us
    dot_general x4, matrix products, chunk_pass(): jnp.einsum('grd,grf->gdf', rows, gate_delta, preferred_element_type=jnp.f...  27.5 us
    all_to_all x4, starting transfers between devices, gather(): lax.all_to_all(jnp.stack([piece] * lax.axis_size('fsdp')), 'fsdp', 0, 0)  27.5 us
    all_to_all x4, local copies, waits for them, and re-layouts, gather(): lax.all_to_all(jnp.stack([piece] * lax.axis_size('fsdp')), 'fsdp', 0, 0)  26.3 us
    dot_general x4, matrix products, chunk_pass(): jnp.einsum('grd,grf->gdf', rows, up_delta, preferred_element_type=jnp.flo...  23.6 us
    dot_general x4, matrix products, chunk_pass(): jnp.einsum('grd,gdf->grf', rows, up_w, preferred_element_type=jnp.float32)  20.9 us
    dot_general x4, matrix products, chunk_pass(): jnp.einsum('grd,gdf->grf', rows, gate_w, preferred_element_type=jnp.float32)  19.5 us
    all_to_all x1, blocking collectives, on_device(): lax.all_to_all(outgoing, 'expert', split_axis=0, concat_axis=0, tiled=True)  14.6 us
  transfers between devices with their start and end apart: 4, of which 4 were waited for; matrix products, arithmetic and copies ran while one was open for 14% of the time, Pallas kernels for 0%

profile of v1, /device:TPU:4, one launch (start us, length us, event | category | flops | bytes accessed | tf_op | source)
XLA Modules:
  0.0 470.5 jit_solution(4766998902174002769)
XLA Ops:
  3.5 14.6 %all_to_all.24 = bf16[4,2,24,2048]{3,2,1,0:T(8,128)(2,1)S(1)} all-to-all(bf16[4,2,24,2048]{3,2,1,0:T(8,128)(2,1)S(1)} %bitcast.56), channel_id=1, replica_groups=mesh['expert'=4,'fsdp'=32] {'expert'}, dimensions={0} | all-to-all | bytes 1572864 | tf_op jit(solution)/shard_map/all_to_all | solution.py:43
  18.2 3.5 stack.6
  21.6 10.7 %all-to-all-start.2 = ((bf16[32,2,24,2048]{3,2,1,0:T(8,128)(2,1)}), bf16[32,2,24,2048]{3,2,1,0:T(8,128)(2,1)}, u32[]{:S(2)}, u32[]{:S(2)}) async-start(bf16[32,2,24,2048]{3,2,1,0:T(8,128)(2,1)} %stack.6), calls=%async_computation.2 | async-start | bytes 12582912 | tf_op jit(solution)/shard_map/all_to_all | solution.py:49
  32.3 88.0 %all-to-all-done.2 = bf16[32,2,24,2048]{3,2,1,0:T(8,128)(2,1)} async-done(((bf16[32,2,24,2048]{3,2,1,0:T(8,128)(2,1)}), bf16[32,2,24,2048]{3,2,1,0:T(8,128)(2,1)}, u32[]{:S(2)}, u32[]{:S(2)}) %all-to-all-start.2) | async-done | bytes 6291488 | tf_op jit(solution)/shard_map/all_to_all | solution.py:49
  120.3 6.6 %copy.23 = bf16[32,2,24,2048]{3,2,0,1:T(8,128)(2,1)} copy(bf16[32,2,24,2048]{3,2,1,0:T(8,128)(2,1)} %all-to-all-done.2) | data formatting | bytes 12582912 | tf_op jit(solution)/shard_map/all_to_all | solution.py:49
  129.5 304.3 %while.22 = (s32[]{:T(128)}, bf16[2,768,2048]{2,1,0:T(8,128)(2,1)}, bf16[2,3072,256]{2,1,0:T(8,128)(2,1)}, f32[2,2048,256]{1,2,0:T(8,128)}, f32[2,2048,256]{1,2,...) while((s32[]{:T(128)}, bf16[2,768,2048]{2,1,0:T(8,128)(2,1)}, ...), condition=%wide.region_3.4_spmd.clone, body=%wide.region_2.3_spmd.clone.sunk | while | flops 6456082432 | bytes 136118656 | solution.py:69
  132.9 5.0 %all-to-all-start = ((bf16[32,2,24,2048]{3,2,1,0:T(8,128)(2,1)}), bf16[32,2,24,2048]{3,2,1,0:T(8,128)(2,1)}, u32[]{:S(2)}, u32[]{:S(2)}) async-start(bf16[32,2,24,2048]{3,2,1,0:T(8,128)(2,1)} %stack.9), calls=%async_computation | async-start | bytes 12582912 | tf_op jit(solution)/shard_map/while/body/eval_jaxpr/all_to_all | solution.py:49
  137.9 4.7 %fusion.68 = f32[2,768,256]{2,1,0:T(8,128)S(1)} fusion(bf16[2,768,2048]{2,1,0:T(8,128)(2,1)} %get-tuple-element.356, bf16[2,2048,256]{2,1,0:T(8,128)(2,1)S(1)} %get-tuple-element.375), kind=kOutput, calls=%fused_computation.52.clone.1 | convolution fusion | flops 1610612736 | bytes 9961472 | tf_op jit(solution)/shard_map/while/body/eval_jaxpr/grd,gdf->grf/dot_general | solution.py:10
  142.7 5.8 %fusion.69 = (bf16[2,3072,256]{2,1,0:T(8,128)(2,1)}, f32[2,768,256]{2,1,0:T(8,128)S(1)}) fusion(bf16[2,3072,256]{2,1,0:T(8,128)(2,1)} %get-tuple-element.357, s32[]{:T(128)S(6)} %select_n.61, f32[2,768,256]{2,1,0:T(8,128)S(1)} %fusion.68, bf16[2,768,2048]{2,1,0:T(8,128)(2,1)} %get-tuple-element.356, bf16[2,2048,256]{2,1,0:T(8,128)(2,1)S(1)} %copy-done.7), kind=kOutput, calls=%fused_computation.11.clone.1 | convolution fusion | flops 1612972032 | bytes 12320772 | tf_op jit(solution)/shard_map/while/body/eval_jaxpr/grd,gdf->grf/dot_general | solution.py:11
  148.6 4.2 bitcast_add_fusion.5
  152.7 4.5 bitcast_add_fusion.4
  157.2 65.6 %all-to-all-done = bf16[32,2,24,2048]{3,2,1,0:T(8,128)(2,1)} async-done(((bf16[32,2,24,2048]{3,2,1,0:T(8,128)(2,1)}), bf16[32,2,24,2048]{3,2,1,0:T(8,128)(2,1)}, u32[]{:S(2)}, u32[]{:S(2)}) %all-to-all-start) | async-done | bytes 6291488 | tf_op jit(solution)/shard_map/while/body/eval_jaxpr/all_to_all | solution.py:49
  222.8 6.6 %copy.33 = bf16[32,2,24,2048]{3,2,0,1:T(8,128)(2,1)} copy(bf16[32,2,24,2048]{3,2,1,0:T(8,128)(2,1)} %all-to-all-done) | data formatting | bytes 12582912 | tf_op jit(solution)/shard_map/while/body/eval_jaxpr/all_to_all | solution.py:49
  232.8 5.9 %all-to-all-start = ((bf16[32,2,24,2048]{3,2,1,0:T(8,128)(2,1)}), bf16[32,2,24,2048]{3,2,1,0:T(8,128)(2,1)}, u32[]{:S(2)}, u32[]{:S(2)}) async-start(bf16[32,2,24,2048]{3,2,1,0:T(8,128)(2,1)} %stack.9), calls=%async_computation | async-start | bytes 12582912 | tf_op jit(solution)/shard_map/while/body/eval_jaxpr/all_to_all | solution.py:49
  238.7 4.7 %fusion.68 = f32[2,768,256]{2,1,0:T(8,128)S(1)} fusion(bf16[2,768,2048]{2,1,0:T(8,128)(2,1)} %get-tuple-element.356, bf16[2,2048,256]{2,1,0:T(8,128)(2,1)S(1)} %get-tuple-element.375), kind=kOutput, calls=%fused_computation.52.clone.1 | convolution fusion | flops 1610612736 | bytes 9961472 | tf_op jit(solution)/shard_map/while/body/eval_jaxpr/grd,gdf->grf/dot_general | solution.py:10
  243.4 5.8 %fusion.69 = (bf16[2,3072,256]{2,1,0:T(8,128)(2,1)}, f32[2,768,256]{2,1,0:T(8,128)S(1)}) fusion(bf16[2,3072,256]{2,1,0:T(8,128)(2,1)} %get-tuple-element.357, s32[]{:T(128)S(6)} %select_n.61, f32[2,768,256]{2,1,0:T(8,128)S(1)} %fusion.68, bf16[2,768,2048]{2,1,0:T(8,128)(2,1)} %get-tuple-element.356, bf16[2,2048,256]{2,1,0:T(8,128)(2,1)S(1)} %copy-done.7), kind=kOutput, calls=%fused_computation.11.clone.1 | convolution fusion | flops 1612972032 | bytes 12320772 | tf_op jit(solution)/shard_map/while/body/eval_jaxpr/grd,gdf->grf/dot_general | solution.py:11
  249.3 6.4 %bitcast_add_fusion.5 = f32[2,2048,256]{1,2,0:T(8,128)} fusion(f32[2,2048,256]{1,2,0:T(8,128)} %get-tuple-element.359, bf16[2,768,2048]{2,1,0:T(8,128)(2,1)S(1)} %bitcast.52, pred[]{:T(512)S(6)} %compare.14, bf16[2,3072,256]{2,1,0:T(8,128)(2,1)S(1)} %copy-done.5, s32[]{:T(128)S(6)} %select_n.61, f32[2,768,256]{2,1,0:T(8,128)S(1)} %fusion.68), kind=kOutput, calls=%fused_computation.clone.1 | convolution fusion | flops 1615462400 | bytes 17039364 | tf_op jit(solution)/shard_map/while/body/eval_jaxpr/grd,grf->gdf/dot_general | solution.py:19
  255.7 6.7 %bitcast_add_fusion.4 = f32[2,2048,256]{1,2,0:T(8,128)} fusion(f32[2,2048,256]{1,2,0:T(8,128)} %get-tuple-element.358, bf16[2,768,2048]{2,1,0:T(8,128)(2,1)S(1)} %bitcast.52, pred[]{:T(512)S(6)} %compare.14, f32[2,768,256]{2,1,0:T(8,128)S(1)} %get-tuple-element.340, f32[2,768,256]{2,1,0:T(8,128)S(1)} %fusion.68, ...), kind=kOutput, calls=%fused_computation.1.clone.1 | convolution fusion | flops 1617035264 | bytes 18612228 | tf_op jit(solution)/shard_map/while/body/eval_jaxpr/grd,grf->gdf/dot_general | solution.py:18
  262.3 62.1 %all-to-all-done = bf16[32,2,24,2048]{3,2,1,0:T(8,128)(2,1)} async-done(((bf16[32,2,24,2048]{3,2,1,0:T(8,128)(2,1)}), bf16[32,2,24,2048]{3,2,1,0:T(8,128)(2,1)}, u32[]{:S(2)}, u32[]{:S(2)}) %all-to-all-start) | async-done | bytes 6291488 | tf_op jit(solution)/shard_map/while/body/eval_jaxpr/all_to_all | solution.py:49
  324.4 6.6 %copy.33 = bf16[32,2,24,2048]{3,2,0,1:T(8,128)(2,1)} copy(bf16[32,2,24,2048]{3,2,1,0:T(8,128)(2,1)} %all-to-all-done) | data formatting | bytes 12582912 | tf_op jit(solution)/shard_map/while/body/eval_jaxpr/all_to_all | solution.py:49
  334.4 5.9 %all-to-all-start = ((bf16[32,2,24,2048]{3,2,1,0:T(8,128)(2,1)}), bf16[32,2,24,2048]{3,2,1,0:T(8,128)(2,1)}, u32[]{:S(2)}, u32[]{:S(2)}) async-start(bf16[32,2,24,2048]{3,2,1,0:T(8,128)(2,1)} %stack.9), calls=%async_computation | async-start | bytes 12582912 | tf_op jit(solution)/shard_map/while/body/eval_jaxpr/all_to_all | solution.py:49
  340.4 4.7 %fusion.68 = f32[2,768,256]{2,1,0:T(8,128)S(1)} fusion(bf16[2,768,2048]{2,1,0:T(8,128)(2,1)} %get-tuple-element.356, bf16[2,2048,256]{2,1,0:T(8,128)(2,1)S(1)} %get-tuple-element.375), kind=kOutput, calls=%fused_computation.52.clone.1 | convolution fusion | flops 1610612736 | bytes 9961472 | tf_op jit(solution)/shard_map/while/body/eval_jaxpr/grd,gdf->grf/dot_general | solution.py:10
  345.1 5.8 %fusion.69 = (bf16[2,3072,256]{2,1,0:T(8,128)(2,1)}, f32[2,768,256]{2,1,0:T(8,128)S(1)}) fusion(bf16[2,3072,256]{2,1,0:T(8,128)(2,1)} %get-tuple-element.357, s32[]{:T(128)S(6)} %select_n.61, f32[2,768,256]{2,1,0:T(8,128)S(1)} %fusion.68, bf16[2,768,2048]{2,1,0:T(8,128)(2,1)} %get-tuple-element.356, bf16[2,2048,256]{2,1,0:T(8,128)(2,1)S(1)} %copy-done.7), kind=kOutput, calls=%fused_computation.11.clone.1 | convolution fusion | flops 1612972032 | bytes 12320772 | tf_op jit(solution)/shard_map/while/body/eval_jaxpr/grd,gdf->grf/dot_general | solution.py:11
  351.0 6.4 %bitcast_add_fusion.5 = f32[2,2048,256]{1,2,0:T(8,128)} fusion(f32[2,2048,256]{1,2,0:T(8,128)} %get-tuple-element.359, bf16[2,768,2048]{2,1,0:T(8,128)(2,1)S(1)} %bitcast.52, pred[]{:T(512)S(6)} %compare.14, bf16[2,3072,256]{2,1,0:T(8,128)(2,1)S(1)} %copy-done.5, s32[]{:T(128)S(6)} %select_n.61, f32[2,768,256]{2,1,0:T(8,128)S(1)} %fusion.68), kind=kOutput, calls=%fused_computation.clone.1 | convolution fusion | flops 1615462400 | bytes 17039364 | tf_op jit(solution)/shard_map/while/body/eval_jaxpr/grd,grf->gdf/dot_general | solution.py:19
  357.4 6.7 %bitcast_add_fusion.4 = f32[2,2048,256]{1,2,0:T(8,128)} fusion(f32[2,2048,256]{1,2,0:T(8,128)} %get-tuple-element.358, bf16[2,768,2048]{2,1,0:T(8,128)(2,1)S(1)} %bitcast.52, pred[]{:T(512)S(6)} %compare.14, f32[2,768,256]{2,1,0:T(8,128)S(1)} %get-tuple-element.340, f32[2,768,256]{2,1,0:T(8,128)S(1)} %fusion.68, ...), kind=kOutput, calls=%fused_computation.1.clone.1 | convolution fusion | flops 1617035264 | bytes 18612228 | tf_op jit(solution)/shard_map/while/body/eval_jaxpr/grd,grf->gdf/dot_general | solution.py:18
  364.0 63.1 %all-to-all-done = bf16[32,2,24,2048]{3,2,1,0:T(8,128)(2,1)} async-done(((bf16[32,2,24,2048]{3,2,1,0:T(8,128)(2,1)}), bf16[32,2,24,2048]{3,2,1,0:T(8,128)(2,1)}, u32[]{:S(2)}, u32[]{:S(2)}) %all-to-all-start) | async-done | bytes 6291488 | tf_op jit(solution)/shard_map/while/body/eval_jaxpr/all_to_all | solution.py:49
  427.2 6.6 %copy.33 = bf16[32,2,24,2048]{3,2,0,1:T(8,128)(2,1)} copy(bf16[32,2,24,2048]{3,2,1,0:T(8,128)(2,1)} %all-to-all-done) | data formatting | bytes 12582912 | tf_op jit(solution)/shard_map/while/body/eval_jaxpr/all_to_all | solution.py:49
  433.8 5.5 %copy.27 = f32[2,2048,256]{2,1,0:T(8,128)} copy(f32[2,2048,256]{1,2,0:T(8,128)} %get-tuple-element.229) | data formatting | bytes 8388608 | tf_op jit(solution)/shard_map/while | solution.py:69
  439.3 5.3 %fusion.36 = f32[2,768,256]{2,1,0:T(8,128)S(1)} fusion(bf16[2,768,2048]{2,1,0:T(8,128)(2,1)} %get-tuple-element.227, bf16[2,2048,256]{2,1,0:T(8,128)(2,1)} %param.9), kind=kOutput, calls=%fused_computation.53 | convolution fusion | flops 1610612736 | bytes 9961472 | tf_op jit(solution)/shard_map/grd,gdf->grf/dot_general | solution.py:10
  445.2 6.7 %convolution_add_fusion = f32[2,2048,256]{2,1,0:T(8,128)} fusion(f32[2,2048,256]{2,1,0:T(8,128)S(1)} %copy-done.2, bf16[2,768,2048]{2,1,0:T(8,128)(2,1)S(1)} %bitcast.55, bf16[2,3072,256]{2,1,0:T(8,128)(2,1)} %get-tuple-element.387, f32[2,768,256]{2,1,0:T(8,128)S(1)} %fusion.36), kind=kOutput, calls=%fused_computation.20 | convolution fusion | flops 1614413824 | bytes 17039360 | tf_op jit(solution)/shard_map/grd,grf->gdf/dot_general | solution.py:19
  455.3 5.5 %copy.25 = f32[2,2048,256]{2,1,0:T(8,128)} copy(f32[2,2048,256]{1,2,0:T(8,128)} %get-tuple-element.228) | data formatting | bytes 8388608 | tf_op jit(solution)/shard_map/while | solution.py:69
  460.8 9.7 %convolution_add_fusion.1 = f32[2,2048,256]{2,1,0:T(8,128)} fusion(f32[2,2048,256]{2,1,0:T(8,128)} %copy.25, bf16[2,768,2048]{2,1,0:T(8,128)(2,1)} %get-tuple-element.227, f32[2,768,256]{2,1,0:T(8,128)} %get-tuple-element.281, f32[2,768,256]{2,1,0:T(8,128)S(1)} %copy-done.4, bf16[2,3072,256]{2,1,0:T(8,128)(2,1)} %get-tuple-element.387), kind=kOutput, calls=%fused_computation.21 | convolution fusion | flops 1615986688 | bytes 18612224 | tf_op jit(solution)/shard_map/grd,grf->gdf/dot_general | solution.py:18
  (62 shorter events, 19.7 us)
Async XLA Ops:
  0.6 2.5 copy-start
  21.6 98.7 %all-to-all-start.2 = ((bf16[32,2,24,2048]{3,2,1,0:T(8,128)(2,1)}), bf16[32,2,24,2048]{3,2,1,0:T(8,128)(2,1)}, u32[]{:S(2)}, u32[]{:S(2)}) async-start(bf16[32,2,24,2048]{3,2,1,0:T(8,128)(2,1)} %stack.6), calls=%async_computation.2 | async-start | bytes 12582912 | tf_op jit(solution)/shard_map/all_to_all | solution.py:49
  126.9 2.6 copy-start.6
  132.9 89.9 %all-to-all-start = ((bf16[32,2,24,2048]{3,2,1,0:T(8,128)(2,1)}), bf16[32,2,24,2048]{3,2,1,0:T(8,128)(2,1)}, u32[]{:S(2)}, u32[]{:S(2)}) async-start(bf16[32,2,24,2048]{3,2,1,0:T(8,128)(2,1)} %stack.9), calls=%async_computation | async-start | bytes 12582912 | tf_op jit(solution)/shard_map/while/body/eval_jaxpr/all_to_all | solution.py:49
  137.9 4.8 %copy-start.7 = (bf16[2,2048,256]{2,1,0:T(8,128)(2,1)S(1)}, bf16[2,2048,256]{2,1,0:T(8,128)(2,1)}, u32[]{:S(2)}) copy-start(bf16[2,2048,256]{2,1,0:T(8,128)(2,1)} %get-tuple-element.376) | copy-start | bytes 6291460 | tf_op jit(solution)/shard_map/while
  137.9 10.6 %slice-start = ((s8[6291456]{0:T(1024)(128)(4,1)}), s8[4194304]{0:T(1024)(128)(4,1)S(1)}, s32[]{:S(2)}) async-start(s8[6291456]{0:T(1024)(128)(4,1)} %bitcast.51), calls=%async_computation.3 | async-start | bytes 8388608 | tf_op jit(solution)/shard_map/while
  142.7 5.9 %slice-start.1 = ((s8[6291456]{0:T(1024)(128)(4,1)}), s8[2097152]{0:T(1024)(128)(4,1)S(1)}, s32[]{:S(2)}) async-start(s8[6291456]{0:T(1024)(128)(4,1)} %bitcast.51), calls=%async_computation.4 | async-start | bytes 4194304 | tf_op jit(solution)/shard_map/while
  142.7 5.9 %copy-start.5 = (bf16[2,3072,256]{2,1,0:T(8,128)(2,1)S(1)}, bf16[2,3072,256]{2,1,0:T(8,128)(2,1)}, u32[]{:S(2)}) copy-start(bf16[2,3072,256]{2,1,0:T(8,128)(2,1)} %get-tuple-element.377) | copy-start | bytes 9437188 | tf_op jit(solution)/shard_map/while
  232.8 91.7 %all-to-all-start = ((bf16[32,2,24,2048]{3,2,1,0:T(8,128)(2,1)}), bf16[32,2,24,2048]{3,2,1,0:T(8,128)(2,1)}, u32[]{:S(2)}, u32[]{:S(2)}) async-start(bf16[32,2,24,2048]{3,2,1,0:T(8,128)(2,1)} %stack.9), calls=%async_computation | async-start | bytes 12582912 | tf_op jit(solution)/shard_map/while/body/eval_jaxpr/all_to_all | solution.py:49
  238.7 4.8 %copy-start.7 = (bf16[2,2048,256]{2,1,0:T(8,128)(2,1)S(1)}, bf16[2,2048,256]{2,1,0:T(8,128)(2,1)}, u32[]{:S(2)}) copy-start(bf16[2,2048,256]{2,1,0:T(8,128)(2,1)} %get-tuple-element.376) | copy-start | bytes 6291460 | tf_op jit(solution)/shard_map/while
  238.7 10.6 %slice-start = ((s8[6291456]{0:T(1024)(128)(4,1)}), s8[4194304]{0:T(1024)(128)(4,1)S(1)}, s32[]{:S(2)}) async-start(s8[6291456]{0:T(1024)(128)(4,1)} %bitcast.51), calls=%async_computation.3 | async-start | bytes 8388608 | tf_op jit(solution)/shard_map/while
  243.4 5.9 %slice-start.1 = ((s8[6291456]{0:T(1024)(128)(4,1)}), s8[2097152]{0:T(1024)(128)(4,1)S(1)}, s32[]{:S(2)}) async-start(s8[6291456]{0:T(1024)(128)(4,1)} %bitcast.51), calls=%async_computation.4 | async-start | bytes 4194304 | tf_op jit(solution)/shard_map/while
  243.4 5.9 %copy-start.5 = (bf16[2,3072,256]{2,1,0:T(8,128)(2,1)S(1)}, bf16[2,3072,256]{2,1,0:T(8,128)(2,1)}, u32[]{:S(2)}) copy-start(bf16[2,3072,256]{2,1,0:T(8,128)(2,1)} %get-tuple-element.377) | copy-start | bytes 9437188 | tf_op jit(solution)/shard_map/while
  334.4 92.8 %all-to-all-start = ((bf16[32,2,24,2048]{3,2,1,0:T(8,128)(2,1)}), bf16[32,2,24,2048]{3,2,1,0:T(8,128)(2,1)}, u32[]{:S(2)}, u32[]{:S(2)}) async-start(bf16[32,2,24,2048]{3,2,1,0:T(8,128)(2,1)} %stack.9), calls=%async_computation | async-start | bytes 12582912 | tf_op jit(solution)/shard_map/while/body/eval_jaxpr/all_to_all | solution.py:49
  340.4 4.8 %copy-start.7 = (bf16[2,2048,256]{2,1,0:T(8,128)(2,1)S(1)}, bf16[2,2048,256]{2,1,0:T(8,128)(2,1)}, u32[]{:S(2)}) copy-start(bf16[2,2048,256]{2,1,0:T(8,128)(2,1)} %get-tuple-element.376) | copy-start | bytes 6291460 | tf_op jit(solution)/shard_map/while
  340.4 10.6 %slice-start = ((s8[6291456]{0:T(1024)(128)(4,1)}), s8[4194304]{0:T(1024)(128)(4,1)S(1)}, s32[]{:S(2)}) async-start(s8[6291456]{0:T(1024)(128)(4,1)} %bitcast.51), calls=%async_computation.3 | async-start | bytes 8388608 | tf_op jit(solution)/shard_map/while
  345.1 5.9 %slice-start.1 = ((s8[6291456]{0:T(1024)(128)(4,1)}), s8[2097152]{0:T(1024)(128)(4,1)S(1)}, s32[]{:S(2)}) async-start(s8[6291456]{0:T(1024)(128)(4,1)} %bitcast.51), calls=%async_computation.4 | async-start | bytes 4194304 | tf_op jit(solution)/shard_map/while
  345.1 5.9 %copy-start.5 = (bf16[2,3072,256]{2,1,0:T(8,128)(2,1)S(1)}, bf16[2,3072,256]{2,1,0:T(8,128)(2,1)}, u32[]{:S(2)}) copy-start(bf16[2,3072,256]{2,1,0:T(8,128)(2,1)} %get-tuple-element.377) | copy-start | bytes 9437188 | tf_op jit(solution)/shard_map/while
  433.8 10.9 %slice-start.2 = ((s8[6291456]{0:T(1024)(128)(4,1)}), s8[2097152]{0:T(1024)(128)(4,1)S(1)}, s32[]{:S(2)}) async-start(s8[6291456]{0:T(1024)(128)(4,1)} %bitcast.54), calls=%async_computation.5 | async-start | bytes 4194304
  439.3 5.4 %slice-start.3 = ((s8[6291456]{0:T(1024)(128)(4,1)}), s8[4194304]{0:T(1024)(128)(4,1)S(1)}, s32[]{:S(2)}) async-start(s8[6291456]{0:T(1024)(128)(4,1)} %bitcast.54), calls=%async_computation.6 | async-start | bytes 8388608
  439.3 5.9 %copy-start.2 = (f32[2,2048,256]{2,1,0:T(8,128)S(1)}, f32[2,2048,256]{2,1,0:T(8,128)}, u32[]{:S(2)}) copy-start(f32[2,2048,256]{2,1,0:T(8,128)} %copy.27) | copy-start | bytes 12582916
  445.2 6.7 %copy-start.3 = (f32[2,768,256]{2,1,0:T(8,128)}, f32[2,768,256]{2,1,0:T(8,128)S(1)}, u32[]{:S(2)}) copy-start(f32[2,768,256]{2,1,0:T(8,128)S(1)} %fusion.36) | copy-start | bytes 4718596
  445.2 6.7 %copy-start.8 = (bf16[2,2048,256]{2,1,0:T(8,128)(2,1)S(1)}, bf16[2,2048,256]{2,1,0:T(8,128)(2,1)}, u32[]{:S(2)}) copy-start(bf16[2,2048,256]{2,1,0:T(8,128)(2,1)} %get-tuple-element.389) | copy-start | bytes 6291460
  455.3 5.5 %copy-start.4 = (f32[2,768,256]{2,1,0:T(8,128)S(1)}, f32[2,768,256]{2,1,0:T(8,128)}, u32[]{:S(2)}) copy-start(f32[2,768,256]{2,1,0:T(8,128)} %copy-done.3) | copy-start | bytes 4718596
  460.8 9.7 %copy-start.1 = (bf16[128,2048]{1,0:T(8,128)(2,1)S(1)}, bf16[128,2048]{1,0:T(8,128)(2,1)}, u32[]{:S(2)}) copy-start(bf16[128,2048]{1,0:T(8,128)(2,1)} %param.7) | copy-start | bytes 1572868
